TPU v7x, 32 devices: a whole 2x2x4 slice. The times are simulated.
32 devices in a mesh: groups: 2 (over y), wide: 4 (over z), ctx: 4 (over x, core).
Axes of the slice: x: 2, y: 2, z: 4, core: 2. Of those that a mesh axis runs over, the one named last changes fastest.
Arguments:
- queries: bfloat16 [4096, 6144], P(('groups', 'ctx'), 'wide'), parts along dimension 0, may hold values from -48 to 48
- key_rows: bfloat16 [4096, 1024], P(('groups', 'ctx')), parts along dimension 0, may hold values from -48 to 48
- value_head_rows: bfloat16 [4096, 1024], P(('groups', 'ctx')), parts along dimension 0, may hold values from -18 to 18
- residual: bfloat16 [4096, 6144], P(('groups', 'ctx'), 'wide'), parts along dimension 0, may hold values from -48 to 48
- out_weight: bfloat16 [6144, 6144], P('wide'), may hold values from -0.109375 to 0.109375
- norm_gain: bfloat16 [6144], P('wide'), may hold values from 0.25 to 1.75
- router_weight: bfloat16 [6144, 8], P('wide'), may hold values from -0.078125 to 0.078125
- gate_weight: bfloat16 [6144, 8192], P('wide', 'ctx'), may hold values from -0.078125 to 0.078125
- up_weight: bfloat16 [6144, 8192], P('wide', 'ctx'), may hold values from -0.078125 to 0.078125
- down_weight: bfloat16 [8192, 6144], P('ctx', 'wide'), may hold values from -0.0625 to 0.0625
- expert_ids: int32 [4096, 2], P('groups'), parts along dimension 0, may hold values from 0 to 7, as said below
- slot_ids: int32 [4096, 2], P('groups'), parts along dimension 0, may hold values from -1 to 639, as said below
Outputs:
- layer_out: bfloat16 [4096, 6144], P(('groups', 'ctx'), 'wide'), parts along dimension 0
There are 2 independent parts, one for each index of `groups`. A program takes and returns all parts, laid end to end along the dimension named above; an argument that names none is the same for every part. Nothing has to cross between parts.
Inputs may be any that keep to these rules, and one draw needn't show every extreme that they name: `expert_ids`: each row names 2 different experts; expert 0 is named by at least 704 rows, so its buffer is full in every draw. `slot_ids`: the rows naming one expert take its buffer rows 0, 1, 2 and so on in the order of positions (for one position, the earlier column first); once 640 rows are taken, further choices of that expert hold -1. Rows of one expert's buffer are never shared.
All inputs are finite; a program needn't handle non-finite values.
Results may differ from a plain program's by a relative error of at most 0.015.
Values may be sent and summed in bfloat16 or wider, within the bound.
No kernel may reach another device: no remote copies, remote signals or barrier semaphores. Data moves between devices by JAX's collectives and lax.ppermute only.
A program may use at most 192 MiB of HBM per device.

v0:
```python
import math
import jax
import jax.numpy as jnp
from jax import lax
from jax.sharding import PartitionSpec as P

D = 6144
QUERY_HEADS = 48
KEY_VALUE_HEADS = 8
HEAD_SIZE = 128
NEG_FILL = -1e30
EPSILON = 1e-05


def token_slots(expert_ids, slot_ids, capacity):
    in_window = jnp.logical_and(expert_ids == 0, slot_ids >= 0)
    picked = jnp.max(jnp.where(in_window, slot_ids, -1), axis=1)
    return jnp.where(picked >= 0, picked, capacity)


def other_experts(expert_ids, slot_of_token, capacity):
    partner = jnp.sum(expert_ids, axis=1)
    return jnp.zeros((capacity,), jnp.int32).at[slot_of_token].set(partner, mode="drop")


def expert_hidden(gate_sum, up_sum, square_sum, logit_sum, slot_other, model_width):
    inverse_rms = lax.rsqrt(square_sum / model_width + EPSILON)
    gate_value = gate_sum * inverse_rms[:, None]
    up_value = up_sum * inverse_rms[:, None]
    logit_value = logit_sum * inverse_rms[:, None]
    columns = jnp.arange(logit_value.shape[1], dtype=jnp.int32)
    partner_logit = jnp.sum(
        jnp.where(columns[None, :] == slot_other[:, None], logit_value, 0.0), axis=1
    )
    mixing = jax.nn.sigmoid(logit_value[:, 0] - partner_logit)
    return (jax.nn.silu(gate_value) * up_value * mixing[:, None]).astype(jnp.bfloat16)


def local(
    queries,
    key_rows,
    value_head_rows,
    residual,
    out_weight,
    norm_gain,
    router_weight,
    gate_weight,
    up_weight,
    down_weight,
    expert_ids,
    slot_ids,
):
    ctx_count = lax.axis_size("ctx")
    wide_index = lax.axis_index("wide")
    ctx_index = lax.axis_index("ctx")
    rows_local = queries.shape[0]
    heads_local = queries.shape[1] // HEAD_SIZE
    query_group_width = QUERY_HEADS // KEY_VALUE_HEADS
    shared_heads = max(1, heads_local // query_group_width)
    per_shared = heads_local // shared_heads
    first_shared = wide_index * heads_local // query_group_width
    key_used = lax.dynamic_slice_in_dim(
        key_rows, first_shared * HEAD_SIZE, shared_heads * HEAD_SIZE, 1
    )
    value_used = lax.dynamic_slice_in_dim(
        value_head_rows, first_shared * HEAD_SIZE, shared_heads * HEAD_SIZE, 1
    )
    query_blocks = queries.reshape(rows_local, shared_heads, per_shared, HEAD_SIZE)
    query_pos = ctx_index * rows_local + jnp.arange(rows_local, dtype=jnp.int32)
    last_query = ctx_index * rows_local + rows_local - 1
    scale_factor = 1.0 / math.sqrt(HEAD_SIZE)
    start_state = (
        jnp.full((shared_heads, per_shared, rows_local), -jnp.inf, jnp.float32),
        jnp.zeros((shared_heads, per_shared, rows_local), jnp.float32),
        jnp.zeros((shared_heads, per_shared, rows_local, HEAD_SIZE), jnp.float32),
    )
    pieces = (
        lax.all_gather(key_used, "ctx", axis=0, tiled=True),
        lax.all_gather(value_used, "ctx", axis=0, tiled=True),
    )

    def update(state):
        running_max, running_sum, running_acc = state
        key_piece = pieces[0].reshape(-1, shared_heads, HEAD_SIZE)
        value_piece = pieces[1].reshape(-1, shared_heads, HEAD_SIZE)
        scores = (
            jnp.einsum(
                "skqd,rkd->kqsr", query_blocks, key_piece, preferred_element_type=jnp.float32
            )
            * scale_factor
        )
        key_pos = jnp.arange(key_piece.shape[0], dtype=jnp.int32)
        allowed = (key_pos[None, :] <= query_pos[:, None])[None, None, :, :]
        masked = jnp.where(allowed, scores, NEG_FILL)
        new_max = jnp.max(masked, axis=-1)
        weights = jnp.where(allowed, jnp.exp(masked - new_max[..., None]), 0.0)
        decay = jnp.exp(running_max - new_max)
        new_sum = running_sum * decay + jnp.sum(weights, axis=-1)
        added = jnp.einsum(
            "kqsr,rkd->kqsd",
            weights.astype(jnp.bfloat16),
            value_piece,
            preferred_element_type=jnp.float32,
        )
        return (new_max, new_sum, running_acc * decay[..., None] + added)

    final_max, final_sum, final_acc = lax.cond(
        jnp.int32(0) > last_query, lambda state: state, update, start_state
    )
    attended = final_acc / final_sum[..., None]
    attended = (
        jnp.transpose(attended, (2, 0, 1, 3))
        .reshape(rows_local, heads_local * HEAD_SIZE)
        .astype(jnp.bfloat16)
    )
    partial_out = jnp.dot(attended, out_weight, preferred_element_type=jnp.float32)
    head_sum = lax.psum_scatter(
        partial_out.astype(jnp.bfloat16), "wide", scatter_dimension=1, tiled=True
    ).astype(jnp.float32)
    resid = (residual.astype(jnp.float32) + head_sum).astype(jnp.bfloat16)
    seq_len = rows_local * ctx_count
    capacity = seq_len * 5 // 16
    width_local = resid.shape[1]
    slot_of_token = token_slots(expert_ids, slot_ids, capacity)
    slot_other = other_experts(expert_ids, slot_of_token, capacity)
    buffer = (
        jnp.zeros((capacity, width_local), jnp.bfloat16)
        .at[slot_of_token]
        .set(lax.all_gather(resid, "ctx", axis=0, tiled=True), mode="drop")
    )
    buffer_wide = buffer.astype(jnp.float32)
    square_part = jnp.sum(buffer_wide * buffer_wide, axis=1)
    scaled = (buffer_wide * norm_gain.astype(jnp.float32)[None, :]).astype(jnp.bfloat16)
    gate_part = jnp.dot(scaled, gate_weight, preferred_element_type=jnp.float32)
    up_part = jnp.dot(scaled, up_weight, preferred_element_type=jnp.float32)
    logit_part = jnp.dot(scaled, router_weight, preferred_element_type=jnp.float32)
    gate_sum, up_sum, square_sum, logit_sum = (
        lax.psum(gate_part.astype(jnp.bfloat16), "wide").astype(jnp.float32),
        lax.psum(up_part.astype(jnp.bfloat16), "wide").astype(jnp.float32),
        lax.psum(square_part.astype(jnp.bfloat16), "wide").astype(jnp.float32),
        lax.psum(logit_part.astype(jnp.bfloat16), "wide").astype(jnp.float32),
    )
    hidden = expert_hidden(gate_sum, up_sum, square_sum, logit_sum, slot_other, D)
    expert_part = jnp.dot(hidden, down_weight, preferred_element_type=jnp.float32)
    expert_pad = jnp.concatenate([expert_part, jnp.zeros((1, width_local), jnp.float32)], axis=0)
    moe_rows = lax.psum_scatter(
        jnp.take(expert_pad, slot_of_token, axis=0).astype(jnp.bfloat16),
        "ctx",
        scatter_dimension=0,
        tiled=True,
    ).astype(jnp.float32)
    return (resid.astype(jnp.float32) + moe_rows).astype(jnp.bfloat16)


def solution(mesh):
    placed = (
        P(("groups", "ctx"), "wide"),
        P(("groups", "ctx"), None),
        P(("groups", "ctx"), None),
        P(("groups", "ctx"), "wide"),
        P("wide", None),
        P("wide"),
        P("wide", None),
        P("wide", "ctx"),
        P("wide", "ctx"),
        P("ctx", "wide"),
        P("groups", None),
        P("groups", None),
    )
    return jax.shard_map(
        local, mesh=mesh, in_specs=placed, out_specs=P(("groups", "ctx"), "wide"), check_vma=False
    )
```

profile of v0, /device:TPU:0, one launch (start us, length us, event | category | flops | bytes accessed | tf_op | source)
XLA Modules:
  0.0 613.0 jit_solution(8369827461181199514)
XLA Ops:
  6.5 1.2 copy-done
  7.8 0.7 constant_dynamic-slice_fusion.1
  8.6 1.7 constant_dynamic-slice_fusion
  10.3 18.0 %all-gather.4.cloned.1.call-done = bf16[2048,256]{1,0:T(8,128)(2,1)} async-done(((bf16[512,256]{1,0:T(8,128)(2,1)}), bf16[2048,256]{1,0:T(8,128)(2,1)}) %all-gather.4.cloned.1.call-update) | async-done | bytes 1048592 | tf_op jit(solution)/shard_map/all_gather | solution.py:78
  28.3 18.3 %all-gather.6.cloned.1.call-done = bf16[2048,256]{1,0:T(8,128)(2,1)} async-done(((bf16[512,256]{1,0:T(8,128)(2,1)}), bf16[2048,256]{1,0:T(8,128)(2,1)}) %all-gather.6.cloned.1.call-update) | async-done | bytes 1048592 | tf_op jit(solution)/shard_map/all_gather | solution.py:79
  46.6 75.7 %conditional.1 = (f32[2,6,512]{2,1,0:T(8,128)S(1)}, f32[2,6,512,128]{2,3,1,0:T(8,128)}) conditional(s32[]{:T(128)} %convert_element_type.76, (s32[]{:T(128)}, s32[512]{0:T(512)S(1)}, bf16[2048,256]{1,0:T(8,128)(2,1)}, bf16[512,1536]{1,0:T(8,128)(2,1)}, bf16[2048,256]{1,0:T(8,128)(2,1)}) %tuple.13, () %tuple.14), branch_computations={%region_0.3_spmd, %region_3.4_spmd} | conditional | flops 6607870464 | bytes 180058160 | solution.py:107
  46.6 0.8 iota_compare_fusion
  47.5 1.7 copy.28
  49.2 2.1 reshape.71
  51.3 21.1 %fusion = (f32[2,6,512]{2,1,0:T(8,128)S(1)}, f32[2,2048,512,6]{2,1,3,0:T(8,128)}) fusion(pred[512,2048]{0,1:T(8,128)(4,1)S(1)} %iota_compare_fusion, bf16[512,2,6,128]{0,3,2,1:T(8,128)(2,1)S(1)} %bitcast.29, bf16[2048,2,128,1]{2,1,0,3:T(2,128)(2,1)} %bitcast.30), kind=kOutput, calls=%fused_computation.5 | convolution fusion | flops 3258968064 | bytes 54026240 | tf_op jit(solution)/shard_map/cond/branch_0_fun/skqd,rkd->kqsr/dot_general | solution.py:87
  72.4 22.0 %fusion.2 = f32[2,6,512]{2,1,0:T(8,128)S(1)} fusion(f32[2,2048,512,6]{2,1,3,0:T(8,128)} %get-tuple-element.49, f32[2,6,512]{2,1,0:T(8,128)S(1)} %get-tuple-element.48, pred[512,2048]{0,1:T(8,128)(4,1)S(1)} %iota_compare_fusion), kind=kLoop, calls=%fused_computation.7 | loop fusion | flops 62908416 | bytes 51429376 | tf_op jit(solution)/shard_map/cond/branch_0_fun/reduce_sum | solution.py:98
  94.4 0.3 reshape.73
  94.7 24.0 %fusion.6 = f32[2,6,512,128]{3,2,1,0:T(8,128)} fusion(f32[2,2048,512,6]{2,1,3,0:T(8,128)} %get-tuple-element.49, f32[2,6,512]{2,1,0:T(8,128)S(1)} %get-tuple-element.48, pred[512,2048]{0,1:T(8,128)(4,1)S(1)} %iota_compare_fusion, f32[2,6,512]{2,1,0:T(8,128)S(1)} %get-tuple-element.46, bf16[2048,2,128,1]{2,1,0,3:T(2,128)(2,1)S(1)} %bitcast.32), kind=kOutput, calls=%fused_computation.11 | convolution fusion | flops 3284926464 | bytes 55623680 | tf_op jit(solution)/shard_map/cond/branch_0_fun/kqsr,rkd->kqsd/dot_general | solution.py:99
  118.8 3.5 copy.38
  122.3 2.3 divide_convert_fusion
  124.7 15.7 %convolution_convert_fusion = bf16[512,6144]{1,0:T(8,128)(2,1)} fusion(bf16[512,1536]{0,1:T(8,128)(2,1)S(1)} %bitcast.31, bf16[1536,6144]{1,0:T(8,128)(2,1)} %param.18), kind=kOutput, calls=%fused_computation.22 | convolution fusion | flops 9666822144 | bytes 26738688 | tf_op jit(solution)/shard_map/dot_general | solution.py:116
  140.5 110.8 %reduce-scatter.3.cloned.1.call-done = bf16[512,1536]{1,0:T(8,128)(2,1)} async-done(((bf16[512,6144]{1,0:T(8,128)(2,1)}), bf16[512,1536]{1,0:T(8,128)(2,1)}) %reduce-scatter.3.cloned.1.call-update) | async-done | bytes 1572880 | tf_op jit(solution)/shard_map/reduce_scatter | solution.py:117
  251.3 2.9 add_convert_fusion.1
  254.4 46.9 %all-gather.8.cloned.1.call-done = bf16[2048,1536]{1,0:T(8,128)(2,1)} async-done(((bf16[512,1536]{1,0:T(8,128)(2,1)}), bf16[2048,1536]{1,0:T(8,128)(2,1)}) %all-gather.8.cloned.1.call-update) | async-done | bytes 6291472 | tf_op jit(solution)/shard_map/all_gather | solution.py:129
  301.3 11.4 %scatter_custom_fusion = bf16[640,1536]{1,0:T(8,128)(2,1)S(1)} fusion(s32[2048]{0:T(1024)S(1)} %bitcast.35, bf16[2048,1536]{1,0:T(8,128)(2,1)} %all-gather.8.cloned.1.call-done, bf16[]{:T(256)} %constant.48.clone.1), kind=kCustom, calls=%fused_computation.36 | custom fusion | bytes 1966592 | tf_op jit(solution)/shard_map/scatter | solution.py:129
  312.8 8.5 %convolution_convert_fusion.1 = bf16[640,2048]{1,0:T(8,128)(2,1)} fusion(bf16[1536,2048]{1,0:T(8,128)(2,1)} %param.22, bf16[640,1536]{1,0:T(8,128)(2,1)S(1)} %scatter_custom_fusion, f32[1536]{0:T(1024)S(1)} %convert_element_type.85), kind=kOutput, calls=%fused_computation.28 | convolution fusion | flops 4030791680 | bytes 10885120 | tf_op jit(solution)/shard_map/dot_general | solution.py:135
  321.2 8.2 %convolution_convert_fusion.2 = bf16[640,2048]{1,0:T(8,128)(2,1)} fusion(bf16[1536,2048]{1,0:T(8,128)(2,1)} %param.21, bf16[640,1536]{1,0:T(8,128)(2,1)S(1)} %scatter_custom_fusion, f32[1536]{0:T(1024)S(1)} %convert_element_type.85), kind=kOutput, calls=%fused_computation.29 | convolution fusion | flops 4030791680 | bytes 10885120 | tf_op jit(solution)/shard_map/dot_general | solution.py:134
  329.6 8.0 %scatter_custom_fusion.1 = s32[640]{0:T(1024)S(1)} fusion(s32[2048]{0:T(1024)S(1)} %bitcast.36, s32[2048]{0:T(1024)S(1)} %get-tuple-element.40, s32[]{:T(128)} %constant.22.clone.1), kind=kCustom, calls=%fused_computation.54 | custom fusion | bytes 2564 | tf_op jit(solution)/shard_map/scatter | solution.py:23
  337.7 0.5 fusion.17
  338.1 0.6 fusion.23
  338.7 19.9 %all-reduce.1 = (bf16[640]{0:T(1024)(128)(2,1)S(1)}, bf16[640,8]{0,1:T(8,128)(2,1)S(1)}) all-reduce(bf16[640]{0:T(1024)(128)(2,1)S(1)} %fusion.17, bf16[640,8]{0,1:T(8,128)(2,1)S(1)} %fusion.23), channel_id=1, replica_groups=mesh['groups'=2,'wide'=4,'ctx'=4] {'wide'}, use_global_device_ids=true, to_apply=%region_9.10 | all-reduce | flops 5760 | bytes 23040 | tf_op jit(solution)/shard_map/psum | solution.py:140
  358.7 160.5 %all-reduce.5.cloned.1.call-done = (bf16[640,2048]{1,0:T(8,128)(2,1)}, bf16[640,2048]{1,0:T(8,128)(2,1)}) async-done(((bf16[640,2048]{1,0:T(8,128)(2,1)}, bf16[640,2048]{1,0:T(8,128)(2,1)}), (bf16[640,2048]{1,0:T(8,128)(2,1)}, bf16[640,2048]{1,0:T(8,128)(2,1)})) %all-reduce.5.cloned.1.call-update) | async-done | bytes 5242896 | tf_op jit(solution)/shard_map/psum | solution.py:139
  519.2 9.2 %fusion.18 = bf16[640,1536]{1,0:T(8,128)(2,1)S(1)} fusion(bf16[2048,1536]{1,0:T(8,128)(2,1)} %param.23, bf16[640,2048]{1,0:T(8,128)(2,1)} %get-tuple-element.44, bf16[640,2048]{1,0:T(8,128)(2,1)} %get-tuple-element.45, f32[640]{0:T(1024)S(1)} %divide_reduce_fusion, f32[640]{0:T(1024)S(1)} %add_rsqrt_fusion), kind=kOutput, calls=%fused_computation.33 | convolution fusion | flops 4040949760 | bytes 13505536 | tf_op jit(solution)/shard_map/dot_general | solution.py:144
  528.5 10.1 %gather_fusion = bf16[2048,1536]{1,0:T(8,128)(2,1)} fusion(bf16[641,1536]{1,0:T(8,128)(2,1)S(1)} %concatenate.3, s32[2048]{0:T(1024)S(1)} %broadcast_clamp_fusion), kind=kCustom, calls=%fused_computation | custom fusion | bytes 12591104 | tf_op jit(solution)/shard_map/jit(_take)/gather | solution.py:147
  538.7 6.6 %select_convert_fusion = bf16[2048,1536]{1,0:T(8,128)(2,1)} fusion(bf16[2048,1536]{1,0:T(8,128)(2,1)} %gather_fusion, pred[2048]{0:T(1024)(128)(4,1)S(1)} %compare_and_fusion), kind=kLoop, calls=%fused_computation.21 | loop fusion | flops 3145728 | bytes 12584960 | tf_op jit(solution)/shard_map/convert_element_type | solution.py:147
  545.3 58.0 %reduce-scatter.5.cloned.1.call-done = bf16[512,1536]{1,0:T(8,128)(2,1)} async-done(((bf16[2048,1536]{1,0:T(8,128)(2,1)}), bf16[512,1536]{1,0:T(8,128)(2,1)}) %reduce-scatter.5.cloned.1.call-update) | async-done | bytes 1572880 | tf_op jit(solution)/shard_map/reduce_scatter | solution.py:146
  603.2 2.9 add_convert_fusion
  (41 shorter events, 0.7 us)
Async XLA Ops:
  6.5 1.2 copy-start
  6.5 21.8 %all-gather.4.cloned.1.call-start = ((), (), s32[]{:S(2)}) async-start(), calls=%async_computation.2 | async-start | bytes 1310720 | tf_op jit(solution)/shard_map/all_gather | solution.py:78
  8.5 38.1 %all-gather.6.cloned.1.call-start = ((), (), s32[]{:S(2)}) async-start(), calls=%async_computation.3 | async-start | bytes 1310720 | tf_op jit(solution)/shard_map/all_gather | solution.py:79
  10.3 241.0 %reduce-scatter.3.cloned.1.call-start = ((), (), s32[]{:S(2)}) async-start(), calls=%async_computation.4 | async-start | bytes 7864320 | tf_op jit(solution)/shard_map/reduce_scatter | solution.py:117
  72.4 22.0 %copy-start.4 = (bf16[2048,256]{1,0:T(8,128)(2,1)S(1)}, bf16[2048,256]{1,0:T(8,128)(2,1)}, u32[]{:S(2)}) copy-start(bf16[2048,256]{1,0:T(8,128)(2,1)} %get-tuple-element.22) | copy-start | bytes 3145732 | tf_op jit(solution)/shard_map/cond
  140.3 111.0 %copy-start.3 = (bf16[512,1536]{1,0:T(8,128)(2,1)S(1)}, bf16[512,1536]{1,0:T(8,128)(2,1)}, u32[]{:S(2)}) copy-start(bf16[512,1536]{1,0:T(8,128)(2,1)} %param.17) | copy-start | bytes 4718596
  140.4 113.9 %copy-start.7 = (bf16[1536]{0:T(1024)(128)(2,1)S(1)}, bf16[1536]{0:T(1024)(128)(2,1)}, u32[]{:S(2)}) copy-start(bf16[1536]{0:T(1024)(128)(2,1)} %param.19) | copy-start | bytes 9220
  140.4 114.0 %copy-start.5 = (s32[2048,2]{0,1:T(2,128)S(1)}, s32[2048,2]{0,1:T(2,128)}, u32[]{:S(2)}) copy-start(s32[2048,2]{0,1:T(2,128)} %param.24) | copy-start | bytes 49156
  140.4 114.0 %copy-start.6 = (s32[2048,2]{0,1:T(2,128)S(1)}, s32[2048,2]{0,1:T(2,128)}, u32[]{:S(2)}) copy-start(s32[2048,2]{0,1:T(2,128)} %param.25) | copy-start | bytes 49156
  140.4 160.9 %all-gather.8.cloned.1.call-start = ((), (), s32[]{:S(2)}) async-start(), calls=%async_computation.5 | async-start | bytes 7864320 | tf_op jit(solution)/shard_map/all_gather | solution.py:129
  254.3 264.9 %all-reduce.5.cloned.1.call-start = ((), (), s32[]{:S(2)}) async-start(), calls=%async_computation.7 | async-start | bytes 10485760 | tf_op jit(solution)/shard_map/psum | solution.py:139
  329.5 8.6 %copy-start.8 = (bf16[1536,8]{0,1:T(8,128)(2,1)S(1)}, bf16[1536,8]{0,1:T(8,128)(2,1)}, u32[]{:S(2)}) copy-start(bf16[1536,8]{0,1:T(8,128)(2,1)} %param.20) | copy-start | bytes 73732
  329.5 273.7 %reduce-scatter.5.cloned.1.call-start = ((), (), s32[]{:S(2)}) async-start(), calls=%async_computation.6 | async-start | bytes 7864320 | tf_op jit(solution)/shard_map/reduce_scatter | solution.py:146
  545.3 58.0 %copy-start.2 = (bf16[512,1536]{1,0:T(8,128)(2,1)S(1)}, bf16[512,1536]{1,0:T(8,128)(2,1)}, u32[]{:S(2)}) copy-start(bf16[512,1536]{1,0:T(8,128)(2,1)} %add_convert_fusion.1) | copy-start | bytes 4718596
  545.3 60.9 %copy-start.1 = (bf16[512,1024]{1,0:T(8,128)(2,1)S(1)}, bf16[512,1024]{1,0:T(8,128)(2,1)}, u32[]{:S(2)}) copy-start(bf16[512,1024]{1,0:T(8,128)(2,1)} %param.15) | copy-start | bytes 3145732
Sparse Core Ops, SparseCore 0:
  8.9 19.4 all-gather.3
  29.9 16.6 all-gather.5
  140.5 110.7 reduce-scatter.2
  254.4 46.8 all-gather.7
  329.6 189.4 all-reduce.4
  545.4 57.7 reduce-scatter.4
where the time goes:
time: 614 us; the launch traced here: 613 us
  waiting for transfers between devices  413 us (67%)
  matrix products  87.4 us (14%)
  local copies, waits for them, and re-layouts  41.1 us (7%)
  other arithmetic  38.2 us (6%)
  blocking collectives  19.9 us (3%)
  between operations  13.6 us (2%)
    psum x1, waiting for transfers between devices, local(): lax.psum(up_part.astype(jnp.bfloat16), 'wide').astype(jnp.float32)  160 us
    reduce_scatter x1, waiting for transfers between devices, local(): lax.psum_scatter(partial_out.astype(jnp.bfloat16), 'wide', scatter_dimens...  111 us
    reduce_scatter x1, waiting for transfers between devices, local(): lax.psum_scatter(jnp.take(expert_pad, slot_of_token, axis=0).astype(jnp.b...  58 us
    all_gather x1, waiting for transfers between devices, local(): lax.all_gather(resid, 'ctx', axis=0, tiled=True)  46.9 us
    dot_general x1, matrix products, update(): jnp.einsum('kqsr,rkd->kqsd', weights.astype(jnp.bfloat16), value_piece, p...  24 us
    reduce_sum x1, other arithmetic, update(): new_sum = running_sum * decay + jnp.sum(weights, axis=-1)  22 us
    dot_general x1, matrix products, update(): jnp.einsum('skqd,rkd->kqsr', query_blocks, key_piece, preferred_element_t...  21.1 us
    psum x1, blocking collectives, local(): lax.psum(square_part.astype(jnp.bfloat16), 'wide').astype(jnp.float32)  19.9 us
  transfers between devices with their start and end apart: 6, of which 6 were waited for; matrix products, arithmetic and copies ran while one was open for 2% of the time, Pallas kernels for 0%

commit v1 on v0

--- a/solution.py
+++ b/solution.py
@@ -1,3 +1,4 @@
+import functools
 import math
 import jax
 import jax.numpy as jnp
@@ -10,6 +11,39 @@
 HEAD_SIZE = 128
 NEG_FILL = -1e30
 EPSILON = 1e-05
+
+
+def finish_cards(content, array_dim):
+    content = jnp.moveaxis(content, 0, array_dim)
+    r_now = content.shape
+    r2 = content.reshape(
+        *r_now[:array_dim], r_now[array_dim] * r_now[array_dim + 1], *r_now[array_dim + 2 :]
+    )
+    return r2
+
+
+def wait_the_cube(slab_in, row_axis, array_axis):
+    q_n = lax.axis_size(row_axis)
+    steps_seen = [(dev, (dev + 1) % q_n) for dev in range(q_n)]
+    carry, local_out = ([], [])
+    column = [(k0, m) for m, k0 in steps_seen]
+    for q in range(q_n - 1):
+        if q % 2 == 0:
+            carry.append(lax.ppermute(carry[-1] if carry else slab_in, row_axis, steps_seen))
+        else:
+            local_out.append(
+                lax.ppermute(local_out[-1] if local_out else slab_in, row_axis, column)
+            )
+    next_value = jnp.stack([*carry[::-1], slab_in, *local_out])
+    tile_out = len(carry)
+    ready = lax.axis_index(row_axis)
+    moved = ready - tile_out
+    next_value = next_value[(jnp.arange(q_n) - moved) % q_n]
+    response = finish_cards(next_value, array_axis)
+    return response
+
+
+state_sheet = functools.partial(wait_the_cube, row_axis="ctx", array_axis=0)
 
 
 def token_slots(expert_ids, slot_ids, capacity):
@@ -126,7 +160,7 @@
     buffer = (
         jnp.zeros((capacity, width_local), jnp.bfloat16)
         .at[slot_of_token]
-        .set(lax.all_gather(resid, "ctx", axis=0, tiled=True), mode="drop")
+        .set(state_sheet(resid), mode="drop")
     )
     buffer_wide = buffer.astype(jnp.float32)
     square_part = jnp.sum(buffer_wide * buffer_wide, axis=1)

time: 614 us -> 635 us (1.034)
  waiting for transfers between devices: 413 us -> 421 us
  local copies, waits for them, and re-layouts: 41.1 us -> 47.5 us
    ppermute x0 -> x3, waiting for transfers between devices: none -> 53.3 us  [the longest x2 52.8 us: wait_the_cube(): lax.ppermute(carry[-1] if carry else slab_in, row_axis, steps_seen)]
    all_gather x1 -> x0, waiting for transfers between devices: 46.9 us -> none  [local(): lax.all_gather(resid, 'ctx', axis=0, tiled=True)]
    gather x0 -> x1, local copies, waits for them, and re-layouts: none -> 6.4 us  [wait_the_cube(): next_value = next_value[(jnp.arange(q_n) - moved) % q_n]]
  transfers between devices with their start and end apart: 6 -> 8, of which waited for: 6 -> 8; matrix products, arithmetic and copies ran while one was open for 2% -> 2% of each run, Pallas kernels for 0% -> 0%
where the time goes in v1:
time: 635 us; the launch traced here: 634 us
  waiting for transfers between devices  421 us (66%)
  matrix products  87.4 us (14%)
  local copies, waits for them, and re-layouts  47.5 us (7%)
  other arithmetic  43.4 us (7%)
  blocking collectives  18.9 us (3%)
  between operations  13.3 us (2%)
    psum x1, waiting for transfers between devices, local(): lax.psum(up_part.astype(jnp.bfloat16), 'wide').astype(jnp.float32)  163 us
    reduce_scatter x1, waiting for transfers between devices, local(): lax.psum_scatter(partial_out.astype(jnp.bfloat16), 'wide', scatter_dimens...  111 us
    reduce_scatter x1, waiting for transfers between devices, local(): lax.psum_scatter(jnp.take(expert_pad, slot_of_token, axis=0).astype(jnp.b...  58 us
    ppermute x2, waiting for transfers between devices, wait_the_cube(): lax.ppermute(carry[-1] if carry else slab_in, row_axis, steps_seen)  52.8 us
    dot_general x1, matrix products, update(): jnp.einsum('kqsr,rkd->kqsd', weights.astype(jnp.bfloat16), value_piece, p...  24 us
    reduce_sum x1, other arithmetic, update(): new_sum = running_sum * decay + jnp.sum(weights, axis=-1)  22 us
    dot_general x1, matrix products, update(): jnp.einsum('skqd,rkd->kqsr', query_blocks, key_piece, preferred_element_t...  21.1 us
    psum x1, blocking collectives, local(): lax.psum(square_part.astype(jnp.bfloat16), 'wide').astype(jnp.float32)  18.9 us
  transfers between devices with their start and end apart: 8, of which 8 were waited for; matrix products, arithmetic and copies ran while one was open for 2% of the time, Pallas kernels for 0%

profile of v1, /device:TPU:0, one launch (start us, length us, event | category | flops | bytes accessed | tf_op | source)
XLA Modules:
  0.0 634.0 jit_solution(18048706070831572900)
XLA Ops:
  6.5 1.2 copy-done
  8.6 1.7 constant_dynamic-slice_fusion
  10.3 18.0 %all-gather.3.cloned.1.call-done = bf16[2048,256]{1,0:T(8,128)(2,1)} async-done(((bf16[512,256]{1,0:T(8,128)(2,1)}), bf16[2048,256]{1,0:T(8,128)(2,1)}) %all-gather.3.cloned.1.call-update) | async-done | bytes 1048592 | tf_op jit(solution)/shard_map/all_gather | solution.py:112
  28.3 18.3 %all-gather.5.cloned.1.call-done = bf16[2048,256]{1,0:T(8,128)(2,1)} async-done(((bf16[512,256]{1,0:T(8,128)(2,1)}), bf16[2048,256]{1,0:T(8,128)(2,1)}) %all-gather.5.cloned.1.call-update) | async-done | bytes 1048592 | tf_op jit(solution)/shard_map/all_gather | solution.py:113
  46.6 75.7 %conditional.1 = (f32[2,6,512]{2,1,0:T(8,128)S(1)}, f32[2,6,512,128]{2,3,1,0:T(8,128)}) conditional(s32[]{:T(128)} %convert_element_type.76, (s32[]{:T(128)}, s32[512]{0:T(512)S(1)}, bf16[2048,256]{1,0:T(8,128)(2,1)}, bf16[512,1536]{1,0:T(8,128)(2,1)}, bf16[2048,256]{1,0:T(8,128)(2,1)}) %tuple.13, () %tuple.14), branch_computations={%region_0.3_spmd, %region_3.4_spmd} | conditional | flops 6607870464 | bytes 180058160 | solution.py:141
  46.6 0.8 iota_compare_fusion
  47.5 1.7 copy.28
  49.2 2.1 reshape.122
  51.3 21.1 %fusion = (f32[2,6,512]{2,1,0:T(8,128)S(1)}, f32[2,2048,512,6]{2,1,3,0:T(8,128)}) fusion(pred[512,2048]{0,1:T(8,128)(4,1)S(1)} %iota_compare_fusion, bf16[512,2,6,128]{0,3,2,1:T(8,128)(2,1)S(1)} %bitcast.37, bf16[2048,2,128,1]{2,1,0,3:T(2,128)(2,1)} %bitcast.39), kind=kOutput, calls=%fused_computation.6 | convolution fusion | flops 3258968064 | bytes 54026240 | tf_op jit(solution)/shard_map/cond/branch_0_fun/skqd,rkd->kqsr/dot_general | solution.py:121
  72.4 22.0 %fusion.2 = f32[2,6,512]{2,1,0:T(8,128)S(1)} fusion(f32[2,2048,512,6]{2,1,3,0:T(8,128)} %get-tuple-element.49, f32[2,6,512]{2,1,0:T(8,128)S(1)} %get-tuple-element.48, pred[512,2048]{0,1:T(8,128)(4,1)S(1)} %iota_compare_fusion), kind=kLoop, calls=%fused_computation.8 | loop fusion | flops 62908416 | bytes 51429376 | tf_op jit(solution)/shard_map/cond/branch_0_fun/reduce_sum | solution.py:132
  94.7 24.0 %fusion.6 = f32[2,6,512,128]{3,2,1,0:T(8,128)} fusion(f32[2,2048,512,6]{2,1,3,0:T(8,128)} %get-tuple-element.49, f32[2,6,512]{2,1,0:T(8,128)S(1)} %get-tuple-element.48, pred[512,2048]{0,1:T(8,128)(4,1)S(1)} %iota_compare_fusion, f32[2,6,512]{2,1,0:T(8,128)S(1)} %get-tuple-element.46, bf16[2048,2,128,1]{2,1,0,3:T(2,128)(2,1)S(1)} %bitcast.41), kind=kOutput, calls=%fused_computation.12 | convolution fusion | flops 3284926464 | bytes 55623680 | tf_op jit(solution)/shard_map/cond/branch_0_fun/kqsr,rkd->kqsd/dot_general | solution.py:133
  118.8 3.5 copy.38
  122.3 2.3 divide_convert_fusion
  124.7 15.7 %convolution_convert_fusion = bf16[512,6144]{1,0:T(8,128)(2,1)} fusion(bf16[512,1536]{0,1:T(8,128)(2,1)S(1)} %bitcast.40, bf16[1536,6144]{1,0:T(8,128)(2,1)} %param.18), kind=kOutput, calls=%fused_computation.23 | convolution fusion | flops 9666822144 | bytes 26738688 | tf_op jit(solution)/shard_map/dot_general | solution.py:150
  140.4 110.9 %reduce-scatter.3.cloned.1.call-done = bf16[512,1536]{1,0:T(8,128)(2,1)} async-done(((bf16[512,6144]{1,0:T(8,128)(2,1)}), bf16[512,1536]{1,0:T(8,128)(2,1)}) %reduce-scatter.3.cloned.1.call-update) | async-done | bytes 1572880 | tf_op jit(solution)/shard_map/reduce_scatter | solution.py:151
  251.3 2.3 add_convert_fusion.1
  253.7 1.7 collective-permute-start.2
  255.4 33.3 %collective-permute-done = bf16[512,1536]{1,0:T(8,128)(2,1)} collective-permute-done((bf16[512,1536]{1,0:T(8,128)(2,1)S(1)}, bf16[512,1536]{1,0:T(8,128)(2,1)}, u32[]{:S(2)}, u32[]{:S(2)}) %collective-permute-start) | collective-permute-done | bytes 1572896 | tf_op jit(solution)/shard_map/ppermute | solution.py:32
  289.3 19.5 %collective-permute-done.1 = bf16[512,1536]{1,0:T(8,128)(2,1)} collective-permute-done((bf16[512,1536]{1,0:T(8,128)(2,1)}, bf16[512,1536]{1,0:T(8,128)(2,1)}, u32[]{:S(2)}, u32[]{:S(2)}) %collective-permute-start.1) | collective-permute-done | bytes 1572896 | tf_op jit(solution)/shard_map/ppermute | solution.py:32
  308.8 5.9 pad_maximum_fusion
  314.8 6.4 %gather_fusion = bf16[4,512,1536]{2,1,0:T(8,128)(2,1)} fusion(bf16[4,512,1536]{2,1,0:T(8,128)(2,1)} %pad_maximum_fusion, s32[1024]{0:T(1024)S(1)} %pad_clamp_fusion), kind=kCustom, calls=%fused_computation | custom fusion | bytes 12582928 | tf_op jit(solution)/shard_map/gather | solution.py:41
  321.2 11.4 %scatter_custom_fusion = bf16[640,1536]{1,0:T(8,128)(2,1)S(1)} fusion(s32[2048]{0:T(1024)S(1)} %bitcast.44, bf16[2048,1536]{1,0:T(8,128)(2,1)} %bitcast.38, bf16[]{:T(256)} %constant.60.clone.1), kind=kCustom, calls=%fused_computation.38 | custom fusion | bytes 1966592 | tf_op jit(solution)/shard_map/scatter | solution.py:163
  332.6 8.5 %convolution_convert_fusion.1 = bf16[640,2048]{1,0:T(8,128)(2,1)} fusion(bf16[1536,2048]{1,0:T(8,128)(2,1)} %param.22, bf16[640,1536]{1,0:T(8,128)(2,1)S(1)} %scatter_custom_fusion, f32[1536]{0:T(1024)S(1)} %convert_element_type.85), kind=kOutput, calls=%fused_computation.30 | convolution fusion | flops 4030791680 | bytes 10885120 | tf_op jit(solution)/shard_map/dot_general | solution.py:169
  341.1 8.2 %convolution_convert_fusion.2 = bf16[640,2048]{1,0:T(8,128)(2,1)} fusion(bf16[1536,2048]{1,0:T(8,128)(2,1)} %param.21, bf16[640,1536]{1,0:T(8,128)(2,1)S(1)} %scatter_custom_fusion, f32[1536]{0:T(1024)S(1)} %convert_element_type.85), kind=kOutput, calls=%fused_computation.31 | convolution fusion | flops 4030791680 | bytes 10885120 | tf_op jit(solution)/shard_map/dot_general | solution.py:168
  349.4 8.0 %scatter_custom_fusion.1 = s32[640]{0:T(1024)S(1)} fusion(s32[2048]{0:T(1024)S(1)} %bitcast.45, s32[2048]{0:T(1024)S(1)} %get-tuple-element.40, s32[]{:T(128)} %constant.36.clone.1), kind=kCustom, calls=%fused_computation.60 | custom fusion | bytes 2564 | tf_op jit(solution)/shard_map/scatter | solution.py:57
  358.6 18.9 %all-reduce.1 = (bf16[640]{0:T(1024)(128)(2,1)S(1)}, bf16[640,8]{0,1:T(8,128)(2,1)S(1)}) all-reduce(bf16[640]{0:T(1024)(128)(2,1)S(1)} %fusion.17, bf16[640,8]{0,1:T(8,128)(2,1)S(1)} %fusion.23), channel_id=1, replica_groups=mesh['groups'=2,'wide'=4,'ctx'=4] {'wide'}, use_global_device_ids=true, to_apply=%region_9.10 | all-reduce | flops 5760 | bytes 23040 | tf_op jit(solution)/shard_map/psum | solution.py:174
  377.6 162.9 %all-reduce.5.cloned.1.call-done = (bf16[640,2048]{1,0:T(8,128)(2,1)}, bf16[640,2048]{1,0:T(8,128)(2,1)}) async-done(((bf16[640,2048]{1,0:T(8,128)(2,1)}, bf16[640,2048]{1,0:T(8,128)(2,1)}), (bf16[640,2048]{1,0:T(8,128)(2,1)}, bf16[640,2048]{1,0:T(8,128)(2,1)})) %all-reduce.5.cloned.1.call-update) | async-done | bytes 5242896 | tf_op jit(solution)/shard_map/psum | solution.py:173
  540.5 9.2 %fusion.18 = bf16[640,1536]{1,0:T(8,128)(2,1)S(1)} fusion(bf16[2048,1536]{1,0:T(8,128)(2,1)} %param.23, bf16[640,2048]{1,0:T(8,128)(2,1)} %get-tuple-element.44, bf16[640,2048]{1,0:T(8,128)(2,1)} %get-tuple-element.45, f32[640]{0:T(1024)S(1)} %divide_reduce_fusion, f32[640]{0:T(1024)S(1)} %add_rsqrt_fusion), kind=kOutput, calls=%fused_computation.35 | convolution fusion | flops 4040949760 | bytes 13505536 | tf_op jit(solution)/shard_map/dot_general | solution.py:178
  549.8 10.1 %gather_fusion.1 = bf16[2048,1536]{1,0:T(8,128)(2,1)} fusion(bf16[641,1536]{1,0:T(8,128)(2,1)S(1)} %concatenate.3, s32[2048]{0:T(1024)S(1)} %broadcast_clamp_fusion), kind=kCustom, calls=%fused_computation.1 | custom fusion | bytes 12591104 | tf_op jit(solution)/shard_map/jit(_take)/gather | solution.py:181
  560.0 6.6 %select_convert_fusion = bf16[2048,1536]{1,0:T(8,128)(2,1)} fusion(bf16[2048,1536]{1,0:T(8,128)(2,1)} %gather_fusion.1, pred[2048]{0:T(1024)(128)(4,1)S(1)} %compare_and_fusion), kind=kLoop, calls=%fused_computation.22 | loop fusion | flops 3145728 | bytes 12584960 | tf_op jit(solution)/shard_map/convert_element_type | solution.py:181
  566.6 58.0 %reduce-scatter.5.cloned.1.call-done = bf16[512,1536]{1,0:T(8,128)(2,1)} async-done(((bf16[2048,1536]{1,0:T(8,128)(2,1)}), bf16[512,1536]{1,0:T(8,128)(2,1)}) %reduce-scatter.5.cloned.1.call-update) | async-done | bytes 1572880 | tf_op jit(solution)/shard_map/reduce_scatter | solution.py:180
  624.5 2.9 add_convert_fusion
  (48 shorter events, 3.3 us)
Async XLA Ops:
  6.5 1.2 copy-start
  6.5 21.8 %all-gather.3.cloned.1.call-start = ((), (), s32[]{:S(2)}) async-start(), calls=%async_computation.2 | async-start | bytes 1310720 | tf_op jit(solution)/shard_map/all_gather | solution.py:112
  8.5 38.1 %all-gather.5.cloned.1.call-start = ((), (), s32[]{:S(2)}) async-start(), calls=%async_computation.3 | async-start | bytes 1310720 | tf_op jit(solution)/shard_map/all_gather | solution.py:113
  10.3 241.0 %reduce-scatter.3.cloned.1.call-start = ((), (), s32[]{:S(2)}) async-start(), calls=%async_computation.4 | async-start | bytes 7864320 | tf_op jit(solution)/shard_map/reduce_scatter | solution.py:151
  72.4 22.0 %copy-start.4 = (bf16[2048,256]{1,0:T(8,128)(2,1)S(1)}, bf16[2048,256]{1,0:T(8,128)(2,1)}, u32[]{:S(2)}) copy-start(bf16[2048,256]{1,0:T(8,128)(2,1)} %get-tuple-element.22) | copy-start | bytes 3145732 | tf_op jit(solution)/shard_map/cond
  140.3 148.3 %copy-start.7 = (bf16[1536]{0:T(1024)(128)(2,1)S(1)}, bf16[1536]{0:T(1024)(128)(2,1)}, u32[]{:S(2)}) copy-start(bf16[1536]{0:T(1024)(128)(2,1)} %param.19) | copy-start | bytes 9220
  140.3 148.4 %copy-start.5 = (s32[2048,2]{0,1:T(2,128)S(1)}, s32[2048,2]{0,1:T(2,128)}, u32[]{:S(2)}) copy-start(s32[2048,2]{0,1:T(2,128)} %param.24) | copy-start | bytes 49156
  140.4 148.4 %copy-start.6 = (s32[2048,2]{0,1:T(2,128)S(1)}, s32[2048,2]{0,1:T(2,128)}, u32[]{:S(2)}) copy-start(s32[2048,2]{0,1:T(2,128)} %param.25) | copy-start | bytes 49156
  140.4 400.1 %all-reduce.5.cloned.1.call-start = ((), (), s32[]{:S(2)}) async-start(), calls=%async_computation.6 | async-start | bytes 10485760 | tf_op jit(solution)/shard_map/psum | solution.py:173
  253.6 61.2 %copy-start.2 = (bf16[512,1536]{1,0:T(8,128)(2,1)}, bf16[512,1536]{1,0:T(8,128)(2,1)S(1)}, u32[]{:S(2)}) copy-start(bf16[512,1536]{1,0:T(8,128)(2,1)S(1)} %add_convert_fusion.1) | copy-start | bytes 4718596
  253.6 35.1 %collective-permute-start = (bf16[512,1536]{1,0:T(8,128)(2,1)S(1)}, bf16[512,1536]{1,0:T(8,128)(2,1)}, u32[]{:S(2)}, u32[]{:S(2)}) collective-permute-start(bf16[512,1536]{1,0:T(8,128)(2,1)S(1)} %add_convert_fusion.1), channel_id=1, source_target_pairs={{0,1},{1,2},{2,3},{3,0},{4,5},{5,6},{6,7},{7,4},{8,9},{9,10},{10,1... | collective-permute-start | bytes 4718600 | tf_op jit(solution)/shard_map/ppermute | solution.py:32
  253.7 35.7 %collective-permute-start.2 = (bf16[512,1536]{1,0:T(8,128)(2,1)S(1)}, bf16[512,1536]{1,0:T(8,128)(2,1)}, u32[]{:S(2)}, u32[]{:S(2)}) collective-permute-start(bf16[512,1536]{1,0:T(8,128)(2,1)S(1)} %add_convert_fusion.1), channel_id=1, source_target_pairs={{1,0},{2,1},{3,2},{0,3},{5,4},{6,5},{7,6},{4,7},{9,8},{10,9},{11,1... | collective-permute-start | bytes 4718600 | tf_op jit(solution)/shard_map/ppermute | solution.py:35
  288.7 20.2 %collective-permute-start.1 = (bf16[512,1536]{1,0:T(8,128)(2,1)}, bf16[512,1536]{1,0:T(8,128)(2,1)}, u32[]{:S(2)}, u32[]{:S(2)}) collective-permute-start(bf16[512,1536]{1,0:T(8,128)(2,1)} %collective-permute-done), channel_id=1, source_target_pairs={{0,1},{1,2},{2,3},{3,0},{4,5},{5,6},{6,7},{7,4},{8,9},{9,10},{10,1... | collective-permute-start | bytes 4718600 | tf_op jit(solution)/shard_map/ppermute | solution.py:32
  349.4 8.6 %copy-start.8 = (bf16[1536,8]{0,1:T(8,128)(2,1)S(1)}, bf16[1536,8]{0,1:T(8,128)(2,1)}, u32[]{:S(2)}) copy-start(bf16[1536,8]{0,1:T(8,128)(2,1)} %param.20) | copy-start | bytes 73732
  349.4 275.2 %reduce-scatter.5.cloned.1.call-start = ((), (), s32[]{:S(2)}) async-start(), calls=%async_computation.5 | async-start | bytes 7864320 | tf_op jit(solution)/shard_map/reduce_scatter | solution.py:180
  566.5 58.0 %copy-start.3 = (bf16[512,1536]{1,0:T(8,128)(2,1)S(1)}, bf16[512,1536]{1,0:T(8,128)(2,1)}, u32[]{:S(2)}) copy-start(bf16[512,1536]{1,0:T(8,128)(2,1)} %copy-done.2) | copy-start | bytes 4718596
  566.5 60.9 %copy-start.1 = (bf16[512,1024]{1,0:T(8,128)(2,1)S(1)}, bf16[512,1024]{1,0:T(8,128)(2,1)}, u32[]{:S(2)}) copy-start(bf16[512,1024]{1,0:T(8,128)(2,1)} %param.15) | copy-start | bytes 3145732
Sparse Core Ops, SparseCore 0:
  8.9 19.4 all-gather.2
  29.9 16.6 all-gather.4
  140.5 110.7 reduce-scatter.2
  349.5 190.9 all-reduce.4
  566.7 57.7 reduce-scatter.4
